TPU v7x, 32 devices: a whole 2x2x4 slice. The times are simulated.
32 devices in a mesh: groups: 2 (over x), blk: 16 (over z, y, core).
Axes of the slice: x: 2, y: 2, z: 4, core: 2. Of those that a mesh axis runs over, the one named last changes fastest.
Arguments:
- paths: bfloat16 [4096, 512], P(('groups', 'blk')), parts along dimension 0, may hold values from -6 to 6
- deltas: bfloat16 [4096, 512], P(('groups', 'blk')), parts along dimension 0, may hold values from -6 to 6
- payoffs: bfloat16 [4096], P(('groups', 'blk')), parts along dimension 0, may hold values from -6 to 6
- counts: int32 [32, 16], P('groups'), parts along dimension 0, may hold values from 0 to 8, as said below
- w_first: bfloat16 [1024, 1024], P(('groups', 'blk')), parts along dimension 0, may hold values from -0.25 to 0.25
- w_second: bfloat16 [2048, 1024], P(('groups', 'blk')), parts along dimension 0, may hold values from -0.1875 to 0.1875
- w_out: bfloat16 [2048], P('groups'), parts along dimension 0, may hold values from -0.1875 to 0.1875
- mom_first: float32 [1024, 1024], P(('groups', 'blk')), parts along dimension 0, may hold values from -6 to 6
- mom_second: float32 [2048, 1024], P(('groups', 'blk')), parts along dimension 0, may hold values from -6 to 6
- mom_out: float32 [2048], P('groups'), parts along dimension 0, may hold values from -6 to 6
Outputs:
- new_first: float32 [1024, 1024], P(('groups', 'blk')), parts along dimension 0
- new_second: float32 [2048, 1024], P(('groups', 'blk')), parts along dimension 0
- new_out: float32 [2048], P('groups'), parts along dimension 0
There are 2 independent parts, one for each index of `groups`. A program takes and returns all parts, laid end to end along the dimension named above; each array names one. Nothing has to cross between parts.
Inputs may be any that keep to these rules, and one draw needn't show every extreme that they name: Source s hands its valid paths, slot 0 onward, to the trainers in order: counts[s, d] of them to trainer d. Every trainer receives 64 paths or fewer in all, and one receives exactly 64; one source hands 8 to every trainer.
All inputs are finite; a program needn't handle non-finite values.
Results may differ from a plain program's by a relative error of at most 0.00035.
The roundings to bfloat16 on the way count: a program that leaves them out, or rounds other values in their place, can miss the bound.
Values may be sent and summed in bfloat16 or wider, within the bound.
No kernel may reach another device: no remote copies, remote signals or barrier semaphores. Data moves between devices by JAX's collectives and lax.ppermute only.
A program may use at most 64 MiB of HBM per device.

v0:
```python
import jax
import jax.numpy as jnp
from jax import lax
from jax.sharding import PartitionSpec as P


def rows_product(left, right):
    return lax.dot_general(
        left, right, (((0,), (0,)), ((), ())), preferred_element_type=jnp.float32
    )


def twin_terms(x_rows, z_rows, y_rows, mask, w_one, w_two, w_three):
    w_outf = w_three.astype(jnp.float32)
    a_one = jnp.dot(x_rows, w_one, preferred_element_type=jnp.float32)
    s_one = jax.nn.sigmoid(a_one)
    h_one = jax.nn.softplus(a_one).astype(jnp.bfloat16)
    a_two = jnp.dot(h_one, w_two, preferred_element_type=jnp.float32)
    s_two = jax.nn.sigmoid(a_two)
    h_two = jax.nn.softplus(a_two)
    value = jnp.sum(h_two * w_outf[None, :], axis=1)
    g_two = (s_two * w_outf[None, :]).astype(jnp.bfloat16)
    c_one = lax.dot_general(
        g_two, w_two, (((1,), (1,)), ((), ())), preferred_element_type=jnp.float32
    )
    g_one = (c_one * s_one).astype(jnp.bfloat16)
    slope = lax.dot_general(
        g_one, w_one, (((1,), (1,)), ((), ())), preferred_element_type=jnp.float32
    )
    e_value = 2.0 * mask * (value - y_rows.astype(jnp.float32))
    e_slope = (2.0 * mask[:, None] * (slope - z_rows.astype(jnp.float32))).astype(jnp.bfloat16)
    e_gone = jnp.dot(e_slope, w_one, preferred_element_type=jnp.float32)
    e_cone = (e_gone * s_one).astype(jnp.bfloat16)
    e_sone = e_gone * c_one
    e_gtwo = jnp.dot(e_cone, w_two, preferred_element_type=jnp.float32)
    grad_three = jnp.sum(e_gtwo * s_two + e_value[:, None] * h_two, axis=0)
    e_atwo = (
        e_gtwo * w_outf[None, :] * s_two * (1.0 - s_two)
        + e_value[:, None] * w_outf[None, :] * s_two
    ).astype(jnp.bfloat16)
    e_hone = lax.dot_general(
        e_atwo, w_two, (((1,), (1,)), ((), ())), preferred_element_type=jnp.float32
    )
    e_aone = (e_sone * s_one * (1.0 - s_one) + e_hone * s_one).astype(jnp.bfloat16)
    return (e_slope, g_one, e_aone, e_cone, g_two, h_one, e_atwo, grad_three)


def normalized(grad):
    return grad / jnp.sqrt(jnp.mean(grad * grad, axis=-1, keepdims=True) + 1e-06)


def per_device(
    paths, deltas, payoffs, counts, w_first, w_second, w_out, mom_first, mom_second, mom_out
):
    position = lax.axis_index("blk")
    rows_dev = paths.shape[0]
    w_one, w_two = (
        lax.all_gather(w_first, "blk", axis=0, tiled=True),
        lax.all_gather(w_second, "blk", axis=0, tiled=True),
    )
    sending = lax.dynamic_index_in_dim(counts, position, 0, keepdims=False)
    x_rows, z_rows, y_rows = (paths, deltas, payoffs)
    total = jnp.sum(sending)
    mask = (jnp.arange(rows_dev, dtype=jnp.int32) < total).astype(jnp.float32)
    e_slope, g_one, e_aone, e_cone, g_two, h_one, e_atwo, grad_three = twin_terms(
        x_rows, z_rows, y_rows, mask, w_one, w_two, w_out
    )
    grad_one = lax.psum_scatter(
        rows_product(x_rows, e_aone) + rows_product(e_slope, g_one),
        "blk",
        scatter_dimension=0,
        tiled=True,
    )
    grad_two = lax.psum_scatter(
        rows_product(e_cone, g_two) + rows_product(h_one, e_atwo),
        "blk",
        scatter_dimension=0,
        tiled=True,
    )
    grad_out = lax.psum(grad_three, "blk")
    new_first = 0.8 * mom_first + 0.2 * normalized(grad_one)
    new_second = 0.8 * mom_second + 0.2 * normalized(grad_two)
    new_out = 0.8 * mom_out + 0.2 * normalized(grad_out)
    return (new_first, new_second, new_out)


def solution(mesh):
    in_specs = (
        P(("groups", "blk"), None),
        P(("groups", "blk"), None),
        P(("groups", "blk")),
        P("groups", None),
        P(("groups", "blk"), None),
        P(("groups", "blk"), None),
        P("groups"),
        P(("groups", "blk"), None),
        P(("groups", "blk"), None),
        P("groups"),
    )
    out_specs = (P(("groups", "blk"), None), P(("groups", "blk"), None), P("groups"))
    return jax.shard_map(
        per_device, mesh=mesh, in_specs=in_specs, out_specs=out_specs, check_vma=False
    )
```

profile of v0, /device:TPU:0, one launch (start us, length us, event | category | flops | bytes accessed | tf_op | source)
XLA Modules:
  0.0 254.4 jit_solution(2150444523015975469)
XLA Ops:
  8.0 0.7 all-gather.5.cloned.1.call-update
  8.7 0.7 convert_element_type.33
  9.4 1.3 dynamic-slice_reduce_fusion
  11.4 39.5 %all-gather.3.cloned.1.call-done = bf16[512,1024]{1,0:T(8,128)(2,1)} async-done(((bf16[32,1024]{1,0:T(8,128)(2,1)}), bf16[512,1024]{1,0:T(8,128)(2,1)}) %all-gather.3.cloned.1.call-update) | async-done | bytes 1048592 | tf_op jit(solution)/shard_map/all_gather | solution.py:58
  50.9 1.5 fusion.17
  52.4 41.0 %all-gather.5.cloned.1.call-done = bf16[1024,1024]{1,0:T(8,128)(2,1)} async-done(((bf16[64,1024]{1,0:T(8,128)(2,1)}), bf16[1024,1024]{1,0:T(8,128)(2,1)}) %all-gather.5.cloned.1.call-update) | async-done | bytes 2097168 | tf_op jit(solution)/shard_map/all_gather | solution.py:59
  93.4 2.6 %multiply_reduce_fusion.1 = (f32[128]{0:T(128)S(1)}, f32[128,1024]{1,0:T(8,128)S(1)}) fusion(f32[1024]{0:T(1024)S(1)} %convert_element_type.33, bf16[1024,1024]{1,0:T(8,128)(2,1)} %all-gather.5.cloned.1.call-done, f32[128,1024]{1,0:T(8,128)S(1)} %fusion.17), kind=kOutput, calls=%fused_computation.16 | convolution fusion | flops 270401408 | bytes 3150336 | tf_op jit(solution)/shard_map/dot_general | solution.py:18
  96.7 1.7 multiply_convert_fusion.1
  98.9 1.1 multiply_convert_fusion
  100.0 0.9 add_reduce_fusion
  100.9 3.0 %fusion.2 = f32[1024,512]{1,0:T(8,128)S(1)} fusion(bf16[128,512]{1,0:T(8,128)(2,1)S(1)} %copy-done, bf16[128,1024]{1,0:T(8,128)(2,1)S(1)} %get-tuple-element.10, bf16[1024,1024]{1,0:T(8,128)(2,1)} %all-gather.5.cloned.1.call-done, f32[128,1024]{1,0:T(8,128)} %get-tuple-element.14, f32[128,1024]{1,0:T(8,128)} %get-tuple-element.12, f32[128,1024]{1,0:T(8,128)S(1)} %fusion.17), kind=kOutput, calls=%fused_computation.7 | convolution fusion | flops 403963904 | bytes 6160384 | tf_op jit(solution)/shard_map/dot_general | solution.py:8
  103.9 1.8 bitcast_add_fusion
  105.7 2.9 %copy.20 = f32[512,1024]{1,0:T(8,128)} copy(f32[512,1024]{0,1:T(8,128)} %bitcast_add_fusion) | data formatting | bytes 4194304
  108.7 1.0 copy-done.4
  109.7 0.8 fusion.11
  110.5 2.8 %convolution_add_fusion = f32[1024,1024]{1,0:T(8,128)} fusion(f32[1024,1024]{1,0:T(8,128)S(1)} %fusion.11, bf16[128,1024]{1,0:T(8,128)(2,1)S(1)} %get-tuple-element.10, f32[128,1024]{1,0:T(8,128)S(1)} %fusion.17), kind=kOutput, calls=%fused_computation | convolution fusion | flops 270401536 | bytes 9175040 | tf_op jit(solution)/shard_map/dot_general | solution.py:8
  113.3 0.9 copy-done.9
  114.4 31.6 %psum.7 = f32[1024]{0:T(1024)S(1)} all-reduce(f32[1024]{0:T(1024)S(1)} %get-tuple-element.9), channel_id=1, replica_groups=mesh['groups'=2,'blk'=16] {'blk'}, use_global_device_ids=true, to_apply=%region_7.8 | all-reduce | flops 1024 | bytes 8192 | tf_op jit(solution)/shard_map/psum | solution.py:80
  148.0 21.5 %reduce-scatter.7.cloned.1.call-done = f32[32,1024]{1,0:T(8,128)} async-done(((f32[512,1024]{1,0:T(8,128)}), f32[32,1024]{1,0:T(8,128)}) %reduce-scatter.7.cloned.1.call-update) | async-done | bytes 131088
  169.5 1.1 copy.21
  170.9 0.8 copy.18
  171.7 73.3 %reduce-scatter.5.cloned.1.call-done = f32[64,1024]{1,0:T(8,128)} async-done(((f32[1024,1024]{1,0:T(8,128)}), f32[64,1024]{1,0:T(8,128)}) %reduce-scatter.5.cloned.1.call-update) | async-done | bytes 262160 | tf_op jit(solution)/shard_map/reduce_scatter | solution.py:74
  245.0 1.1 multiply_reduce_fusion.2
  246.1 1.8 multiply_add_fusion.1
  (39 shorter events, 4.5 us)
Async XLA Ops:
  7.2 43.7 %copy-start = (bf16[128,512]{1,0:T(8,128)(2,1)S(1)}, bf16[128,512]{1,0:T(8,128)(2,1)}, u32[]{:S(2)}) copy-start(bf16[128,512]{1,0:T(8,128)(2,1)} %param.10) | copy-start | bytes 393220
  7.2 43.7 %all-gather.3.cloned.1.call-start = ((), (), s32[]{:S(2)}) async-start(), calls=%async_computation.2 | async-start | bytes 1114112 | tf_op jit(solution)/shard_map/all_gather | solution.py:58
  7.9 85.4 %all-gather.5.cloned.1.call-start = ((), (), s32[]{:S(2)}) async-start(), calls=%async_computation.3 | async-start | bytes 2228224 | tf_op jit(solution)/shard_map/all_gather | solution.py:59
  8.7 160.8 %reduce-scatter.7.cloned.1.call-start = ((), (), s32[]{:S(2)}) async-start(), calls=%async_computation.5 | async-start | bytes 2228224
  52.4 43.6 %copy-start.11 = (bf16[128]{0:T(256)(128)(2,1)S(1)}, bf16[128]{0:T(256)(128)(2,1)}, u32[]{:S(2)}) copy-start(bf16[128]{0:T(256)(128)(2,1)} %param.12) | copy-start | bytes 772
  93.4 3.3 %copy-start.2 = (bf16[1024,1024]{1,0:T(8,128)(2,1)S(1)}, bf16[1024,1024]{1,0:T(8,128)(2,1)}, u32[]{:S(2)}) copy-start(bf16[1024,1024]{1,0:T(8,128)(2,1)} %all-gather.5.cloned.1.call-done) | copy-start | bytes 6291460
  96.0 4.0 %copy-start.3 = (f32[128,1024]{1,0:T(8,128)}, f32[128,1024]{1,0:T(8,128)S(1)}, u32[]{:S(2)}) copy-start(f32[128,1024]{1,0:T(8,128)S(1)} %get-tuple-element.16) | copy-start | bytes 1572868
  96.7 1.7 copy-start.1
  96.7 1.7 copy-start.8
  100.0 0.9 copy-start.5
  108.6 1.0 copy-start.4
  108.6 1.1 copy-start.6
  108.7 136.4 %reduce-scatter.5.cloned.1.call-start = ((), (), s32[]{:S(2)}) async-start(), calls=%async_computation.4 | async-start | bytes 4456448 | tf_op jit(solution)/shard_map/reduce_scatter | solution.py:74
  113.3 0.9 copy-start.9
  113.3 34.0 %copy-start.10 = (f32[1024]{0:T(1024)S(1)}, f32[1024]{0:T(1024)}, u32[]{:S(2)}) copy-start(f32[1024]{0:T(1024)} %param.19) | copy-start | bytes 12292
  114.2 131.9 %copy-start.7 = (f32[64,1024]{1,0:T(8,128)S(1)}, f32[64,1024]{1,0:T(8,128)}, u32[]{:S(2)}) copy-start(f32[64,1024]{1,0:T(8,128)} %param.18) | copy-start | bytes 786436
Sparse Core Ops, SparseCore 0:
  10.2 40.6 all-gather.2
  53.0 40.3 all-gather.4
  108.8 60.6 reduce-scatter.6
  173.7 71.2 reduce-scatter.4
where the time goes:
time: 255 us; the launch traced here: 254 us
  waiting for transfers between devices  177 us (69%)
  blocking collectives  31.6 us (12%)
  matrix products  16.7 us (7%)
  between operations  14.6 us (6%)
  other arithmetic  7.63 us (3%)
  local copies, waits for them, and re-layouts  6.99 us (3%)
    reduce_scatter x1, waiting for transfers between devices, per_device(): lax.psum_scatter(rows_product(e_cone, g_two) + rows_product(h_one, e_atwo...  73.3 us
    all_gather x1, waiting for transfers between devices, per_device(): lax.all_gather(w_second, 'blk', axis=0, tiled=True)  41 us
    all_gather x1, waiting for transfers between devices, per_device(): lax.all_gather(w_first, 'blk', axis=0, tiled=True)  39.5 us
    psum x1, blocking collectives, per_device(): grad_out = lax.psum(grad_three, 'blk')  31.6 us
    unnamed x5, waiting for transfers between devices  22.9 us
    dot_general x4, matrix products, rows_product(): lax.dot_general(left, right, (((0,), (0,)), ((), ())), preferred_element_...  8.39 us
    unnamed x28, local copies, waits for them, and re-layouts  6.99 us
  transfers between devices with their start and end apart: 4, of which 4 were waited for; matrix products, arithmetic and copies ran while one was open for 4% of the time, Pallas kernels for 0%

commit v1 on v0

--- a/solution.py
+++ b/solution.py
@@ -2,6 +2,28 @@
 import jax.numpy as jnp
 from jax import lax
 from jax.sharding import PartitionSpec as P
+
+
+def joined_along(blocks, dim):
+    dims = list(blocks.shape[1:])
+    dims[dim] *= blocks.shape[0]
+    return jnp.moveaxis(blocks, 0, dim).reshape(dims)
+
+
+def doubled(value, axis):
+    count = lax.axis_size(axis)
+    tiles = value[None]
+    for level in range(count.bit_length() - 1):
+        stride = 1 << level
+        other = lax.ppermute(tiles, axis, [(i, i ^ stride) for i in range(count)])
+        both = jnp.stack([tiles, other])
+        upper = lax.axis_index(axis) >> level & 1
+        tiles = jnp.where(upper == 0, both, both[::-1]).reshape(-1, *value.shape)
+    return tiles
+
+
+def gather_by_bits(value, axis, dim):
+    return joined_along(doubled(value, axis), dim)
 
 
 def rows_product(left, right):
@@ -55,7 +77,7 @@
     position = lax.axis_index("blk")
     rows_dev = paths.shape[0]
     w_one, w_two = (
-        lax.all_gather(w_first, "blk", axis=0, tiled=True),
+        gather_by_bits(w_first, "blk", 0),
         lax.all_gather(w_second, "blk", axis=0, tiled=True),
     )
     sending = lax.dynamic_index_in_dim(counts, position, 0, keepdims=False)

time: 255 us -> 228 us (0.89)
  waiting for transfers between devices: 177 us -> 141 us
  starting transfers between devices: 0.16 us -> 8.15 us
    all_gather x1 -> x0, waiting for transfers between devices: 39.5 us -> none  [per_device(): lax.all_gather(w_first, 'blk', axis=0, tiled=True)]
    ppermute x0 -> x4, waiting for transfers between devices: none -> 38.3 us  [doubled(): other = lax.ppermute(tiles, axis, [(i, i ^ stride) for i in range(count)])]
    all_gather x1, waiting for transfers between devices: 41 us -> 7.28 us  [per_device(): lax.all_gather(w_second, 'blk', axis=0, tiled=True)]
    ppermute x0 -> x4, starting transfers between devices: none -> 8.03 us  [doubled(): other = lax.ppermute(tiles, axis, [(i, i ^ stride) for i in range(count)])]
    unnamed x5 -> x4, waiting for transfers between devices: 22.9 us -> 22.2 us
  transfers between devices with their start and end apart: 4 -> 7, of which waited for: 4 -> 7; matrix products, arithmetic and copies ran while one was open for 4% -> 5% of each run, Pallas kernels for 0% -> 0%
where the time goes in v1:
time: 228 us
  waiting for transfers between devices  141 us (62%)
  blocking collectives  31.9 us (14%)
  matrix products  16.7 us (7%)
  between operations  14.7 us (6%)
  other arithmetic  8.39 us (4%)
  starting transfers between devices  8.15 us (4%)
  local copies, waits for them, and re-layouts  6.98 us (3%)
    reduce_scatter x1, waiting for transfers between devices, per_device(): lax.psum_scatter(rows_product(e_cone, g_two) + rows_product(h_one, e_atwo...  73.5 us
    ppermute x4, waiting for transfers between devices, doubled(): other = lax.ppermute(tiles, axis, [(i, i ^ stride) for i in range(count)])  38.3 us
    psum x1, blocking collectives, per_device(): grad_out = lax.psum(grad_three, 'blk')  31.9 us
    unnamed x4, waiting for transfers between devices  22.2 us
    dot_general x4, matrix products, rows_product(): lax.dot_general(left, right, (((0,), (0,)), ((), ())), preferred_element_...  8.47 us
    ppermute x4, starting transfers between devices, doubled(): other = lax.ppermute(tiles, axis, [(i, i ^ stride) for i in range(count)])  8.03 us
    all_gather x1, waiting for transfers between devices, per_device(): lax.all_gather(w_second, 'blk', axis=0, tiled=True)  7.28 us
    unnamed x28, local copies, waits for them, and re-layouts  6.98 us
  transfers between devices with their start and end apart: 7, of which 7 were waited for; matrix products, arithmetic and copies ran while one was open for 5% of the time, Pallas kernels for 0%

profile of v1, /device:TPU:0, one launch (start us, length us, event | category | flops | bytes accessed | tf_op | source)
XLA Modules:
  0.0 228.1 jit_solution(1540560880228306558)
XLA Ops:
  8.5 1.1 collective-permute-done
  10.5 2.9 %collective-permute-start.1 = (bf16[2,32,1024]{2,1,0:T(8,128)(2,1)S(1)}, bf16[2,32,1024]{2,1,0:T(8,128)(2,1)S(1)}, u32[]{:S(2)}, u32[]{:S(2)}) collective-permute-start(bf16[2,32,1024]{2,1,0:T(8,128)(2,1)S(1)} %get-tuple-element.12), channel_id=1, source_target_pairs={{0,2},{1,3},{2,0},{3,1},{4,6},{5,7},{6,4},{7,5},{8,10},{9,11},{10,... | collective-permute-start | bytes 393224 | tf_op jit(solution)/shard_map/ppermute | solution.py:18
  13.4 3.8 %collective-permute-done.1 = bf16[2,32,1024]{2,1,0:T(8,128)(2,1)S(1)} collective-permute-done((bf16[2,32,1024]{2,1,0:T(8,128)(2,1)S(1)}, bf16[2,32,1024]{2,1,0:T(8,128)(2,1)S(1)}, u32[]{:S(2)}, u32[]{:S(2)}) %collective-permute-start.1) | collective-permute-done | bytes 131104 | tf_op jit(solution)/shard_map/ppermute | solution.py:18
  17.3 1.9 collective-permute-start.2
  19.2 7.5 %collective-permute-done.2 = bf16[4,32,1024]{2,1,0:T(8,128)(2,1)S(1)} collective-permute-done((bf16[4,32,1024]{2,1,0:T(8,128)(2,1)S(1)}, bf16[4,32,1024]{2,1,0:T(8,128)(2,1)S(1)}, u32[]{:S(2)}, u32[]{:S(2)}) %collective-permute-start.2) | collective-permute-done | bytes 262176 | tf_op jit(solution)/shard_map/ppermute | solution.py:18
  26.8 2.7 %collective-permute-start.3 = (bf16[8,32,1024]{2,1,0:T(8,128)(2,1)S(1)}, bf16[8,32,1024]{2,1,0:T(8,128)(2,1)S(1)}, u32[]{:S(2)}, u32[]{:S(2)}) collective-permute-start(bf16[8,32,1024]{2,1,0:T(8,128)(2,1)S(1)} %bitcast.40), channel_id=1, source_target_pairs={{0,8},{1,9},{2,10},{3,11},{4,12},{5,13},{6,14},{7,15},{8,0},{9,1},... | collective-permute-start | bytes 1572872 | tf_op jit(solution)/shard_map/ppermute | solution.py:18
  29.6 1.3 dynamic-slice_reduce_fusion
  31.5 25.9 %collective-permute-done.3 = bf16[8,32,1024]{2,1,0:T(8,128)(2,1)S(1)} collective-permute-done((bf16[8,32,1024]{2,1,0:T(8,128)(2,1)S(1)}, bf16[8,32,1024]{2,1,0:T(8,128)(2,1)S(1)}, u32[]{:S(2)}, u32[]{:S(2)}) %collective-permute-start.3) | collective-permute-done | bytes 524320 | tf_op jit(solution)/shard_map/ppermute | solution.py:18
  58.3 7.3 %all-gather.2.cloned.1.call-done = bf16[1024,1024]{1,0:T(8,128)(2,1)} async-done(((bf16[64,1024]{1,0:T(8,128)(2,1)}), bf16[1024,1024]{1,0:T(8,128)(2,1)}) %all-gather.2.cloned.1.call-update) | async-done | bytes 2097168 | tf_op jit(solution)/shard_map/all_gather | solution.py:81
  65.6 2.9 %multiply_reduce_fusion.1 = (f32[128]{0:T(128)S(1)}, f32[128,1024]{0,1:T(8,128)S(1)}) fusion(f32[1024]{0:T(1024)S(1)} %convert_element_type.33, bf16[1024,1024]{1,0:T(8,128)(2,1)} %all-gather.2.cloned.1.call-done, f32[128,1024]{0,1:T(8,128)S(1)} %convolution_bitcast_fusion), kind=kOutput, calls=%fused_computation.21 | convolution fusion | flops 270401408 | bytes 3150336 | tf_op jit(solution)/shard_map/dot_general | solution.py:40
  68.5 1.6 multiply_convert_fusion.1
  70.7 1.3 multiply_convert_fusion
  72.7 1.4 add_reduce_fusion
  74.1 3.2 %fusion.2 = f32[1024,512]{1,0:T(8,128)S(1)} fusion(bf16[128,512]{1,0:T(8,128)(2,1)S(1)} %copy-done, bf16[1024,1024]{1,0:T(8,128)(2,1)} %all-gather.2.cloned.1.call-done, bf16[128,1024]{0,1:T(8,128)(2,1)S(1)} %get-tuple-element.10, f32[128,1024]{0,1:T(8,128)} %get-tuple-element.16, f32[128,1024]{0,1:T(8,128)} %get-tuple-element.14, ...), kind=kOutput, calls=%fused_computation.9 | convolution fusion | flops 403963904 | bytes 6160384 | tf_op jit(solution)/shard_map/dot_general | solution.py:30
  77.2 1.8 bitcast_add_fusion
  79.0 2.9 %copy.48 = f32[512,1024]{1,0:T(8,128)} copy(f32[512,1024]{0,1:T(8,128)} %bitcast_add_fusion) | data formatting | bytes 4194304
  82.0 1.0 copy-done.3
  83.8 2.7 %convolution_add_fusion = f32[1024,1024]{1,0:T(8,128)} fusion(f32[1024,1024]{1,0:T(8,128)S(1)} %fusion.17, bf16[128,1024]{0,1:T(8,128)(2,1)S(1)} %get-tuple-element.10, f32[128,1024]{0,1:T(8,128)S(1)} %convolution_bitcast_fusion), kind=kOutput, calls=%fused_computation | convolution fusion | flops 270401536 | bytes 9175040 | tf_op jit(solution)/shard_map/dot_general | solution.py:30
  87.7 31.9 %psum.7 = f32[1024]{0:T(1024)S(1)} all-reduce(f32[1024]{0:T(1024)S(1)} %get-tuple-element.9), channel_id=1, replica_groups=mesh['groups'=2,'blk'=16] {'blk'}, use_global_device_ids=true, to_apply=%region_7.8 | all-reduce | flops 1024 | bytes 8192 | tf_op jit(solution)/shard_map/psum | solution.py:102
  121.5 21.5 %reduce-scatter.7.cloned.1.call-done = f32[32,1024]{1,0:T(8,128)} async-done(((f32[512,1024]{1,0:T(8,128)}), f32[32,1024]{1,0:T(8,128)}) %reduce-scatter.7.cloned.1.call-update) | async-done | bytes 131088
  142.9 1.1 copy.49
  145.1 73.5 %reduce-scatter.5.cloned.1.call-done = f32[64,1024]{1,0:T(8,128)} async-done(((f32[1024,1024]{1,0:T(8,128)}), f32[64,1024]{1,0:T(8,128)}) %reduce-scatter.5.cloned.1.call-update) | async-done | bytes 262160 | tf_op jit(solution)/shard_map/reduce_scatter | solution.py:96
  218.7 1.1 multiply_reduce_fusion.2
  219.8 1.8 multiply_add_fusion.1
  (52 shorter events, 9.4 us)
Async XLA Ops:
  7.2 50.7 %copy-start = (bf16[128,512]{1,0:T(8,128)(2,1)S(1)}, bf16[128,512]{1,0:T(8,128)(2,1)}, u32[]{:S(2)}) copy-start(bf16[128,512]{1,0:T(8,128)(2,1)} %param.10) | copy-start | bytes 393220
  7.2 22.4 %copy-start.10 = (bf16[1024]{0:T(1024)(128)(2,1)S(1)}, bf16[1024]{0:T(1024)(128)(2,1)}, u32[]{:S(2)}) copy-start(bf16[1024]{0:T(1024)(128)(2,1)} %param.16) | copy-start | bytes 6148
  7.2 58.4 %all-gather.2.cloned.1.call-start = ((), (), s32[]{:S(2)}) async-start(), calls=%async_computation.2 | async-start | bytes 2228224 | tf_op jit(solution)/shard_map/all_gather | solution.py:81
  7.9 135.0 %reduce-scatter.7.cloned.1.call-start = ((), (), s32[]{:S(2)}) async-start(), calls=%async_computation.4 | async-start | bytes 2228224
  8.0 1.6 collective-permute-start
  10.5 6.8 %collective-permute-start.1 = (bf16[2,32,1024]{2,1,0:T(8,128)(2,1)S(1)}, bf16[2,32,1024]{2,1,0:T(8,128)(2,1)S(1)}, u32[]{:S(2)}, u32[]{:S(2)}) collective-permute-start(bf16[2,32,1024]{2,1,0:T(8,128)(2,1)S(1)} %get-tuple-element.12), channel_id=1, source_target_pairs={{0,2},{1,3},{2,0},{3,1},{4,6},{5,7},{6,4},{7,5},{8,10},{9,11},{10,... | collective-permute-start | bytes 393224 | tf_op jit(solution)/shard_map/ppermute | solution.py:18
  17.3 9.3 %collective-permute-start.2 = (bf16[4,32,1024]{2,1,0:T(8,128)(2,1)S(1)}, bf16[4,32,1024]{2,1,0:T(8,128)(2,1)S(1)}, u32[]{:S(2)}, u32[]{:S(2)}) collective-permute-start(bf16[4,32,1024]{2,1,0:T(8,128)(2,1)S(1)} %bitcast.42), channel_id=1, source_target_pairs={{0,4},{1,5},{2,6},{3,7},{4,0},{5,1},{6,2},{7,3},{8,12},{9,13},{10,... | collective-permute-start | bytes 786440 | tf_op jit(solution)/shard_map/ppermute | solution.py:18
  26.8 30.7 %collective-permute-start.3 = (bf16[8,32,1024]{2,1,0:T(8,128)(2,1)S(1)}, bf16[8,32,1024]{2,1,0:T(8,128)(2,1)S(1)}, u32[]{:S(2)}, u32[]{:S(2)}) collective-permute-start(bf16[8,32,1024]{2,1,0:T(8,128)(2,1)S(1)} %bitcast.40), channel_id=1, source_target_pairs={{0,8},{1,9},{2,10},{3,11},{4,12},{5,13},{6,14},{7,15},{8,0},{9,1},... | collective-permute-start | bytes 1572872 | tf_op jit(solution)/shard_map/ppermute | solution.py:18
  65.6 2.9 %copy-start.1 = (bf16[1024,1024]{1,0:T(8,128)(2,1)S(1)}, bf16[1024,1024]{1,0:T(8,128)(2,1)}, u32[]{:S(2)}) copy-start(bf16[1024,1024]{1,0:T(8,128)(2,1)} %all-gather.2.cloned.1.call-done) | copy-start | bytes 6291460
  68.5 4.2 %copy-start.2 = (f32[128,1024]{0,1:T(8,128)}, f32[128,1024]{0,1:T(8,128)S(1)}, u32[]{:S(2)}) copy-start(f32[128,1024]{0,1:T(8,128)S(1)} %get-tuple-element.18) | copy-start | bytes 1572868
  68.5 1.7 copy-start.7
  70.2 1.8 copy-start.11
  72.0 2.0 copy-start.4
  81.9 1.0 copy-start.3
  81.9 1.1 copy-start.5
  81.9 136.8 %reduce-scatter.5.cloned.1.call-start = ((), (), s32[]{:S(2)}) async-start(), calls=%async_computation.3 | async-start | bytes 4456448 | tf_op jit(solution)/shard_map/reduce_scatter | solution.py:96
  86.6 0.9 copy-start.8
  86.6 34.3 %copy-start.9 = (f32[1024]{0:T(1024)S(1)}, f32[1024]{0:T(1024)}, u32[]{:S(2)}) copy-start(f32[1024]{0:T(1024)} %param.19) | copy-start | bytes 12292
  87.5 132.3 %copy-start.6 = (f32[64,1024]{1,0:T(8,128)S(1)}, f32[64,1024]{1,0:T(8,128)}, u32[]{:S(2)}) copy-start(f32[64,1024]{1,0:T(8,128)} %param.18) | copy-start | bytes 786436
Sparse Core Ops, SparseCore 0:
  10.2 55.3 all-gather.1
  82.1 60.8 reduce-scatter.6
  147.3 71.3 reduce-scatter.4
